TPU v7x, 256 devices: a whole 4x4x8 slice. The times are simulated.
256 devices in a mesh: dom: 64 (over y, z, core), rep: 4 (over x).
Axes of the slice: x: 4, y: 4, z: 8, core: 2. Of those that a mesh axis runs over, the one named last changes fastest.
Arguments:
- x_loader: bfloat16 [131072, 512], P(('dom', 'rep')), may hold values from -6 to 6
- owner_index: int32 [131072], P(('dom', 'rep')), may hold values from 0 to 131071, as said below
- tile_vals: bfloat16 [1024, 12, 128, 128], P(('dom', 'rep')), as said below
- tile_cols: int32 [1024, 12], P(('dom', 'rep')), may hold values from 0 to 1023, as said below
- tile_live: int32 [1024, 12], P(('dom', 'rep')), may hold values from 0 to 1, as said below
- w_self: bfloat16 [512, 512], replicated, may hold values from -0.25 to 0.25
- w_neigh: bfloat16 [512, 512], replicated, may hold values from -3 to 3
- bias: float32 [512], replicated, may hold values from -3 to 3
- cotangent: bfloat16 [131072, 512], P(('dom', 'rep')), may hold values from -6 to 6
Outputs:
- layer_out: bfloat16 [131072, 512], P(('dom', 'rep'))
- grad_features: bfloat16 [131072, 512], P(('dom', 'rep'))
- grad_self: float32 [512, 512], replicated
- grad_neigh: float32 [512, 512], replicated
- grad_bias: float32 [512], replicated
Inputs may be any that keep to these rules, and one draw needn't show every extreme that they name: `owner_index`: A permutation of the 131072 rows. Loader rows are in blocks of 512 in the order of the devices (dom slowest); owner rows likewise. The 512 rows of each loader block with rep index r go to owner blocks of rep index r, 8 rows to each of the 64 partitions. `tile_cols`: partition p holds row tiles p * 16 to (p + 1) * 16 - 1. A column tile of a row tile of partition p lies in partition p or within 4 tiles beyond its edges. W is symmetric: every live slot (t, c) with tiles B is matched by a live slot (c, t) with tiles B^T, a slot with c = t holding a symmetric tile. `tile_live`: live slots are symmetric as stated for tile_cols. `tile_vals`: nonnegative edge weights.
All inputs are finite; a program needn't handle non-finite values.
Results may differ from a plain program's by a relative error of at most 0.0075.
Values may be sent and summed in bfloat16 or wider, within the bound.
No kernel may reach another device: no remote copies, remote signals or barrier semaphores. Data moves between devices by JAX's collectives and lax.ppermute only.
A program may use at most 64 MiB of HBM per device.

v0:
```python
import jax
import jax.numpy as jnp
from jax import lax
from jax.sharding import PartitionSpec as P

HALO_T = 4


def shifted(value, axis, steps):
    count = lax.axis_size(axis)
    first, last = (max(0, -steps), min(count, count - steps))
    return lax.ppermute(value, axis, [(source, source + steps) for source in range(first, last)])


def with_halo(block, sides, width):
    for axis, dim in sides:
        count = lax.axis_size(axis)
        forward = [(i, i + 1) for i in range(count - 1)]
        backward = [(target, source) for source, target in forward]
        low = lax.ppermute(
            lax.slice_in_dim(block, block.shape[dim] - width, None, axis=dim), axis, forward
        )
        high = lax.ppermute(lax.slice_in_dim(block, 0, width, axis=dim), axis, backward)
        block = jnp.concatenate([low, block, high], axis=dim)
    return block


def contract_rows(left, right):
    return lax.dot_general(
        left, right, (((0,), (0,)), ((), ())), preferred_element_type=jnp.float32
    )


def contract_cols(left, right):
    return lax.dot_general(
        left, right, (((1,), (1,)), ((), ())), preferred_element_type=jnp.float32
    )


def pass_rim(values, offset):
    return shifted(values.astype(jnp.bfloat16), "dom", offset).astype(values.dtype)


def shards(
    x_loader, owner_index, tile_vals, tile_cols, tile_live, w_self, w_neigh, bias, cotangent
):
    rows, width = x_loader.shape
    reps = lax.axis_size("rep")
    dom_place = lax.axis_index("dom")
    part_rows = rows * reps
    part_tiles = part_rows // 128
    row_tiles = rows // 128
    rim_rows = HALO_T * 128
    dest = owner_index // part_rows
    order = jnp.argsort(dest, stable=True)
    moved, slot = (
        lax.all_to_all(x_loader[order], "dom", split_axis=0, concat_axis=0, tiled=True),
        lax.all_to_all((owner_index % rows)[order], "dom", split_axis=0, concat_axis=0, tiled=True),
    )
    features = jnp.zeros((rows, width), jnp.bfloat16).at[slot].set(moved)
    first_tile = dom_place * part_tiles - HALO_T
    local_cols = tile_cols - first_tile
    masked = tile_vals * tile_live.astype(jnp.bfloat16)[:, :, None, None]
    degree = 1.0 + jnp.sum(masked, axis=(1, 3), dtype=jnp.float32)
    whole = lax.all_gather(features, "rep", axis=0, tiled=True)
    extended = with_halo(whole, (("dom", 0),), rim_rows)
    picked = extended.reshape(-1, 128, width)[local_cols]
    summed = jnp.einsum("tkab,tkbf->taf", masked, picked, preferred_element_type=jnp.float32)
    agg = (summed / degree[:, :, None]).reshape(rows, width).astype(jnp.bfloat16)
    pre = (
        jnp.dot(features, w_self, preferred_element_type=jnp.float32)
        + jnp.dot(agg, w_neigh, preferred_element_type=jnp.float32)
        + bias
    )
    layer_out = jnp.where(pre > 0, pre, jnp.expm1(jnp.minimum(pre, 0.0))).astype(jnp.bfloat16)
    slope = jnp.where(pre > 0, 1.0, jnp.exp(jnp.minimum(pre, 0.0)))
    dz = (cotangent.astype(jnp.float32) * slope).astype(jnp.bfloat16)
    grad_self, grad_neigh, grad_bias = lax.psum(
        (
            contract_rows(features, dz),
            contract_rows(agg, dz),
            jnp.sum(dz, axis=0, dtype=jnp.float32),
        ),
        ("dom", "rep"),
    )
    scaled = (contract_cols(dz, w_neigh) / degree.reshape(rows, 1)).astype(jnp.bfloat16)
    terms = jnp.einsum(
        "tkab,taf->tkbf",
        masked,
        scaled.reshape(row_tiles, 128, width),
        preferred_element_type=jnp.float32,
    )
    span_tiles = part_tiles + 2 * HALO_T
    selector = (
        local_cols.reshape(-1)[None, :] == jnp.arange(span_tiles, dtype=jnp.int32)[:, None]
    ).astype(jnp.float32)
    buffer = jnp.einsum(
        "en,nbf->ebf", selector, terms.reshape(-1, 128, width), precision=lax.Precision.HIGHEST
    )
    buffer = buffer.reshape(span_tiles * 128, width)
    lower = buffer[:rim_rows]
    upper = buffer[rim_rows + part_rows :]
    core = buffer[rim_rows : rim_rows + part_rows]
    core = core.at[:rim_rows].add(pass_rim(upper, 1))
    core = core.at[part_rows - rim_rows :].add(pass_rim(lower, -1))
    back = lax.psum_scatter(core, "rep", scatter_dimension=0, tiled=True)
    grad_features = (contract_cols(dz, w_self) + back).astype(jnp.bfloat16)
    return (layer_out, grad_features, grad_self, grad_neigh, grad_bias)


def solution(mesh):
    return jax.shard_map(
        shards,
        mesh=mesh,
        in_specs=(
            P(("dom", "rep"), None),
            P(("dom", "rep")),
            P(("dom", "rep"), None, None, None),
            P(("dom", "rep"), None),
            P(("dom", "rep"), None),
            P(),
            P(),
            P(),
            P(("dom", "rep"), None),
        ),
        out_specs=(P(("dom", "rep"), None), P(("dom", "rep"), None), P(), P(), P()),
        check_vma=False,
    )
```

profile of v0, /device:TPU:2, one launch (start us, length us, event | category | flops | bytes accessed | tf_op | source)
XLA Modules:
  0.0 486.7 jit_solution(7837561082085686232)
XLA Ops:
  7.2 0.0 copy-start
  7.2 0.8 add_select_fusion
  8.0 3.8 sort.17
  11.8 3.5 gather_fusion
  15.3 0.0 copy-start.10
  15.3 0.0 copy-start.9
  15.3 0.0 copy-start.3
  15.3 0.7 all_to_all.16
  16.0 12.1 %all-to-all-start = ((s32[64,8,1]{1,2,0:T(1,128)}), s32[64,8,1]{1,2,0:T(1,128)S(1)}, u32[]{:S(2)}, u32[]{:S(2)}) async-start(s32[64,8,1]{1,2,0:T(1,128)} %bitcast), calls=%async_computation | async-start | bytes 65536 | tf_op jit(solution)/shard_map/all_to_all | solution.py:58
  28.1 2.6 gather_fusion.1
  30.7 6.8 %all-to-all-done = s32[64,8,1]{1,2,0:T(1,128)S(1)} async-done(((s32[64,8,1]{1,2,0:T(1,128)}), s32[64,8,1]{1,2,0:T(1,128)S(1)}, u32[]{:S(2)}, u32[]{:S(2)}) %all-to-all-start) | async-done | bytes 2080 | tf_op jit(solution)/shard_map/all_to_all | solution.py:58
  37.5 4.6 all-to-all-start.1
  42.2 0.0 all-gather.2.cloned.1.call-start
  42.2 0.5 broadcast.92
  42.7 0.7 reduce.7
  43.5 0.1 all_to_all.18
  43.6 15.8 %all-to-all-done.1 = bf16[64,8,512]{2,1,0:T(8,128)(2,1)S(1)} async-done(((bf16[64,8,512]{2,1,0:T(8,128)(2,1)}), bf16[64,8,512]{2,1,0:T(8,128)(2,1)S(1)}, u32[]{:S(2)}, u32[]{:S(2)}) %all-to-all-start.1) | async-done | bytes 524320 | tf_op jit(solution)/shard_map/all_to_all | solution.py:57
  59.4 3.2 scatter_custom_fusion
  62.5 0.0 all-gather.2.cloned.1.call-update
  62.6 0.0 reduce-scatter.2.cloned.1.call-start
  62.6 0.1 reshape.147
  62.7 0.5 convert_reduce_fusion
  63.2 29.2 %all-gather.2.cloned.1.call-done = bf16[2048,512]{1,0:T(8,128)(2,1)} async-done(((bf16[512,512]{1,0:T(8,128)(2,1)}), bf16[2048,512]{1,0:T(8,128)(2,1)}) %all-gather.2.cloned.1.call-update) | async-done | bytes 2097168 | tf_op jit(solution)/shard_map/all_gather | solution.py:65
  92.4 2.2 fusion.26
  94.6 2.5 collective-permute-start
  97.2 1.3 collective-permute-start.1
  98.5 0.1 eq.17
  98.6 1.4 fusion.28
  100.0 0.0 collective-permute-done
  100.0 1.9 collective-permute-done.1
  101.9 3.1 pad_maximum_fusion
  105.0 6.8 %gather_fusion.2 = bf16[48,128,512]{2,1,0:T(8,128)(2,1)} fusion(bf16[24,128,512]{2,1,0:T(8,128)(2,1)} %bitcast.50, s32[1024]{0:T(1024)S(1)} %pad_clamp_fusion), kind=kCustom, calls=%fused_computation.2 | custom fusion | bytes 12583104 | tf_op jit(solution)/shard_map/gather | solution.py:67
  111.9 4.0 fusion.5
  115.9 0.0 copy-start.7
  115.9 1.7 convert_reduce_fusion.1
  117.7 0.5 fusion.3
  118.1 1.9 fusion.6
  120.1 12.3 %fusion.27 = (bf16[24,128,512]{2,0,1:T(8,128)(2,1)S(1)}, f32[24,128,512]{2,0,1:T(8,128)S(1)}) fusion(f32[48,128,512]{2,1,0:T(8,128)S(1)} %bitcast.49, s32[48]{0:T(128)S(1)} %eq.17), kind=kOutput, calls=%fused_computation.56 | convolution fusion | flops 907543680 | bytes 22020288 | tf_op jit(solution)/shard_map/en,nbf->ebf/dot_general | solution.py:97
  132.4 0.4 fusion.25
  132.8 0.1 copy.31
  132.9 9.1 %collective-permute-start.2 = (bf16[512,512]{1,0:T(8,128)(2,1)S(1)}, bf16[512,512]{1,0:T(8,128)(2,1)S(1)}, u32[]{:S(2)}, u32[]{:S(2)}) collective-permute-start(bf16[512,512]{1,0:T(8,128)(2,1)S(1)} %bitcast.54), channel_id=1, source_target_pairs={{0,4},{4,8},{8,12},{12,16},{16,20},{20,24},{24,28},{28,32},{32,36}... | collective-permute-start | bytes 1572872 | tf_op jit(solution)/shard_map/ppermute | solution.py:12
  142.0 0.1 copy.32
  142.1 1.3 collective-permute-start.3
  143.4 1.0 slice.78
  144.5 0.3 slice.79
  144.7 4.4 copy.29
  149.1 0.3 copy.30
  149.4 0.0 collective-permute-done.2
  149.5 0.0 copy-start.8
  149.5 1.1 constant_dynamic-update-slice_fusion
  150.6 2.4 fusion.12
  153.0 0.0 reduce-scatter.2.cloned.1.call-update
  153.1 0.0 copy-start.5
  153.1 0.0 all-reduce.3.cloned.1.call-start
  153.1 1.4 fusion.31
  154.6 1.4 fusion.30
  156.0 0.0 all-reduce.3.cloned.1.call-update
  156.0 83.0 %psum.23 = f32[512]{0:T(512)} all-reduce(f32[512]{0:T(512)S(1)} %get-tuple-element.33), channel_id=1, replica_groups=mesh['dom'=64,'rep'=4] {'dom','rep'}, use_global_device_ids=true, to_apply=%region_7.8 | all-reduce | flops 512 | bytes 4096 | tf_op jit(solution)/shard_map/psum | solution.py:78
  239.0 0.5 fusion.29
  239.4 0.0 reduce-scatter.2.cloned.1.call-done
  239.5 2.2 add_convert_fusion
  241.7 234.0 %all-reduce.3.cloned.1.call-done = (f32[512,512]{1,0:T(8,128)}, f32[512,512]{1,0:T(8,128)}) async-done(((f32[512,512]{1,0:T(8,128)}, f32[512,512]{1,0:T(8,128)}), (f32[512,512]{1,0:T(8,128)}, f32[512,512]{1,0:T(8,128)})) %all-reduce.3.cloned.1.call-update) | async-done | bytes 2097168 | tf_op jit(solution)/shard_map/psum | solution.py:78
  475.6 2.3 copy.44
  477.9 2.3 copy.45
  (28 shorter events, 0.1 us)
Async XLA Ops:
  7.2 108.7 %copy-start = (bf16[512,512]{1,0:T(8,128)(2,1)S(1)}, bf16[512,512]{1,0:T(8,128)(2,1)}, u32[]{:S(2)}) copy-start(bf16[512,512]{1,0:T(8,128)(2,1)} %param.19) | copy-start | bytes 1572868
  7.2 20.9 %copy-start.1 = (bf16[512,512]{1,0:T(8,128)(2,1)S(1)}, bf16[512,512]{1,0:T(8,128)(2,1)}, u32[]{:S(2)}) copy-start(bf16[512,512]{1,0:T(8,128)(2,1)} %param.13) | copy-start | bytes 1572868
  15.3 47.4 %copy-start.10 = (s32[4,12]{1,0:T(4,128)S(1)}, s32[4,12]{1,0:T(4,128)}, u32[]{:S(2)}) copy-start(s32[4,12]{1,0:T(4,128)} %param.16) | copy-start | bytes 580
  15.3 47.5 %copy-start.9 = (s32[4,12]{1,0:T(4,128)S(1)}, s32[4,12]{1,0:T(4,128)}, u32[]{:S(2)}) copy-start(s32[4,12]{1,0:T(4,128)} %param.17) | copy-start | bytes 580
  15.3 47.5 %copy-start.3 = (bf16[4,12,128,128]{3,2,1,0:T(8,128)(2,1)S(1)}, bf16[4,12,128,128]{3,2,1,0:T(8,128)(2,1)}, u32[]{:S(2)}) copy-start(bf16[4,12,128,128]{3,2,1,0:T(8,128)(2,1)} %param.15) | copy-start | bytes 4718596
  16.0 21.5 %all-to-all-start = ((s32[64,8,1]{1,2,0:T(1,128)}), s32[64,8,1]{1,2,0:T(1,128)S(1)}, u32[]{:S(2)}, u32[]{:S(2)}) async-start(s32[64,8,1]{1,2,0:T(1,128)} %bitcast), calls=%async_computation | async-start | bytes 65536 | tf_op jit(solution)/shard_map/all_to_all | solution.py:58
  30.7 67.8 %copy-start.4 = (bf16[512,512]{1,0:T(8,128)(2,1)S(1)}, bf16[512,512]{1,0:T(8,128)(2,1)}, u32[]{:S(2)}) copy-start(bf16[512,512]{1,0:T(8,128)(2,1)} %param.18) | copy-start | bytes 1572868
  37.5 21.8 %all-to-all-start.1 = ((bf16[64,8,512]{2,1,0:T(8,128)(2,1)}), bf16[64,8,512]{2,1,0:T(8,128)(2,1)S(1)}, u32[]{:S(2)}, u32[]{:S(2)}) async-start(bf16[64,8,512]{2,1,0:T(8,128)(2,1)} %bitcast.2), calls=%async_computation.1 | async-start | bytes 1048576 | tf_op jit(solution)/shard_map/all_to_all | solution.py:57
  42.2 50.2 %all-gather.2.cloned.1.call-start = ((), (), s32[]{:S(2)}) async-start(), calls=%async_computation.3 | async-start | bytes 2621440 | tf_op jit(solution)/shard_map/all_gather | solution.py:65
  62.5 36.0 %copy-start.2 = (bf16[512,512]{1,0:T(8,128)(2,1)S(1)}, bf16[512,512]{1,0:T(8,128)(2,1)}, u32[]{:S(2)}) copy-start(bf16[512,512]{1,0:T(8,128)(2,1)} %scatter_custom_fusion) | copy-start | bytes 1572868
  62.6 176.9 %reduce-scatter.2.cloned.1.call-start = ((), (), s32[]{:S(2)}) async-start(), calls=%async_computation.4 | async-start | bytes 5242880 | tf_op jit(solution)/shard_map/reduce_scatter | solution.py:106
  94.6 5.3 %collective-permute-start = (bf16[512,512]{1,0:T(8,128)(2,1)}, bf16[512,512]{1,0:T(8,128)(2,1)}, u32[]{:S(2)}, u32[]{:S(2)}) collective-permute-start(bf16[512,512]{1,0:T(8,128)(2,1)} %get-tuple-element.39), channel_id=1, source_target_pairs={{0,4},{4,8},{8,12},{12,16},{16,20},{20,24},{24,28},{28,32},{32,36}... | collective-permute-start | bytes 1572872 | tf_op jit(solution)/shard_map/ppermute | solution.py:20
  97.2 4.7 collective-permute-start.1
  111.8 4.1 copy-start.6
  111.9 4.1 copy-start.11
  111.9 4.1 copy-start.12
  115.9 2.3 copy-start.7
  132.9 16.5 %collective-permute-start.2 = (bf16[512,512]{1,0:T(8,128)(2,1)S(1)}, bf16[512,512]{1,0:T(8,128)(2,1)S(1)}, u32[]{:S(2)}, u32[]{:S(2)}) collective-permute-start(bf16[512,512]{1,0:T(8,128)(2,1)S(1)} %bitcast.54), channel_id=1, source_target_pairs={{0,4},{4,8},{8,12},{12,16},{16,20},{20,24},{24,28},{28,32},{32,36}... | collective-permute-start | bytes 1572872 | tf_op jit(solution)/shard_map/ppermute | solution.py:12
  142.1 8.5 %collective-permute-start.3 = (bf16[512,512]{1,0:T(8,128)(2,1)S(1)}, bf16[512,512]{1,0:T(8,128)(2,1)S(1)}, u32[]{:S(2)}, u32[]{:S(2)}) collective-permute-start(bf16[512,512]{1,0:T(8,128)(2,1)S(1)} %bitcast.53), channel_id=1, source_target_pairs={{4,0},{8,4},{12,8},{16,12},{20,16},{24,20},{28,24},{32,28},{36,32}... | collective-permute-start | bytes 1572872 | tf_op jit(solution)/shard_map/ppermute | solution.py:12
  149.5 3.7 copy-start.8
  153.1 85.9 %copy-start.5 = (bf16[512,512]{1,0:T(8,128)(2,1)S(1)}, bf16[512,512]{1,0:T(8,128)(2,1)}, u32[]{:S(2)}) copy-start(bf16[512,512]{1,0:T(8,128)(2,1)} %param.18) | copy-start | bytes 1572868
  153.1 322.6 %all-reduce.3.cloned.1.call-start = ((), (), s32[]{:S(2)}) async-start(), calls=%async_computation.5 | async-start | bytes 4194304 | tf_op jit(solution)/shard_map/psum | solution.py:78
Sparse Core Ops, SparseCore 0:
  62.7 29.6 all-gather.1
  153.2 52.8 reduce-scatter.1
  213.1 262.4 all-reduce.2
where the time goes:
time: 487 us
  waiting for transfers between devices  288 us (59%)
  blocking collectives  83 us (17%)
  local copies, waits for them, and re-layouts  31.1 us (6%)
  starting transfers between devices  31.1 us (6%)
  matrix products  25.2 us (5%)
  other arithmetic  14.6 us (3%)
  between operations  14.1 us (3%)
    psum x1, waiting for transfers between devices, shards(): lax.psum((contract_rows(features, dz), contract_rows(agg, dz), jnp.sum(dz...  234 us
    psum x1, blocking collectives, shards(): lax.psum((contract_rows(features, dz), contract_rows(agg, dz), jnp.sum(dz...  83 us
    all_gather x1, waiting for transfers between devices, shards(): whole = lax.all_gather(features, 'rep', axis=0, tiled=True)  29.2 us
    all_to_all x1, waiting for transfers between devices, shards(): lax.all_to_all(x_loader[order], 'dom', split_axis=0, concat_axis=0, tiled...  15.8 us
    dot_general x1, matrix products, shards(): jnp.einsum('en,nbf->ebf', selector, terms.reshape(-1, 128, width), precis...  12.3 us
    all_to_all x1, starting transfers between devices, shards(): lax.all_to_all((owner_index % rows)[order], 'dom', split_axis=0, concat_a...  12.1 us
    ppermute x2, starting transfers between devices, shifted(): lax.ppermute(value, axis, [(source, source + steps) for source in range(f...  10.4 us
  transfers between devices with their start and end apart: 9, of which 5 were waited for; matrix products, arithmetic and copies ran while one was open for 4% of the time, Pallas kernels for 0%

commit v1 on v0

--- a/solution.py
+++ b/solution.py
@@ -4,6 +4,11 @@
 from jax.sharding import PartitionSpec as P
 
 HALO_T = 4
+
+
+def exchange_gather(x, axis, along):
+    outgoing = jnp.stack([x] * lax.axis_size(axis))
+    return jnp.concatenate(lax.all_to_all(outgoing, axis, 0, 0), axis=along)
 
 
 def shifted(value, axis, steps):
@@ -62,7 +67,7 @@
     local_cols = tile_cols - first_tile
     masked = tile_vals * tile_live.astype(jnp.bfloat16)[:, :, None, None]
     degree = 1.0 + jnp.sum(masked, axis=(1, 3), dtype=jnp.float32)
-    whole = lax.all_gather(features, "rep", axis=0, tiled=True)
+    whole = exchange_gather(features, "rep", 0)
     extended = with_halo(whole, (("dom", 0),), rim_rows)
     picked = extended.reshape(-1, 128, width)[local_cols]
     summed = jnp.einsum("tkab,tkbf->taf", masked, picked, preferred_element_type=jnp.float32)

time: 487 us -> 453 us (0.930)
  waiting for transfers between devices: 288 us -> 245 us
    psum x1, waiting for transfers between devices: 234 us -> 199 us  [shards(): lax.psum((contract_rows(features, dz), contract_rows(agg, dz), jnp.sum(dz...]
    all_gather x1 -> x0, waiting for transfers between devices: 29.2 us -> none  [shards(): whole = lax.all_gather(features, 'rep', axis=0, tiled=True)]
    all_to_all x0 -> x1, waiting for transfers between devices: none -> 23.2 us  [exchange_gather(): return jnp.concatenate(lax.all_to_all(outgoing, axis, 0, 0), axis=along)]
  transfers between devices with their start and end apart: 9 -> 9, of which waited for: 5 -> 5; matrix products, arithmetic and copies ran while one was open for 4% -> 5% of each run, Pallas kernels for 0% -> 0%
where the time goes in v1:
time: 453 us
  waiting for transfers between devices  245 us (54%)
  blocking collectives  83.4 us (18%)
  starting transfers between devices  35.3 us (8%)
  local copies, waits for them, and re-layouts  30.8 us (7%)
  matrix products  26.2 us (6%)
  between operations  15.8 us (3%)
  other arithmetic  15.7 us (3%)
    psum x1, waiting for transfers between devices, shards(): lax.psum((contract_rows(features, dz), contract_rows(agg, dz), jnp.sum(dz...  199 us
    psum x1, blocking collectives, shards(): lax.psum((contract_rows(features, dz), contract_rows(agg, dz), jnp.sum(dz...  83.4 us
    all_to_all x1, waiting for transfers between devices, exchange_gather(): return jnp.concatenate(lax.all_to_all(outgoing, axis, 0, 0), axis=along)  23.2 us
    all_to_all x1, waiting for transfers between devices, shards(): lax.all_to_all(x_loader[order], 'dom', split_axis=0, concat_axis=0, tiled...  15.8 us
    dot_general x1, matrix products, shards(): jnp.einsum('en,nbf->ebf', selector, terms.reshape(-1, 128, width), precis...  12.3 us
    all_to_all x1, starting transfers between devices, shards(): lax.all_to_all((owner_index % rows)[order], 'dom', split_axis=0, concat_a...  12.1 us
    ppermute x2, starting transfers between devices, shifted(): lax.ppermute(value, axis, [(source, source + steps) for source in range(f...  10.4 us
  transfers between devices with their start and end apart: 9, of which 5 were waited for; matrix products, arithmetic and copies ran while one was open for 5% of the time, Pallas kernels for 0%

profile of v1, /device:TPU:2, one launch (start us, length us, event | category | flops | bytes accessed | tf_op | source)
XLA Modules:
  0.0 452.7 jit_solution(10412210641896423649)
XLA Ops:
  8.0 0.0 copy-start
  8.0 0.8 add_select_fusion
  8.8 3.8 sort.17
  12.6 3.5 gather_fusion
  16.1 0.7 all_to_all.19
  16.8 12.1 %all-to-all-start = ((s32[64,8,1]{1,2,0:T(1,128)}), s32[64,8,1]{1,2,0:T(1,128)S(1)}, u32[]{:S(2)}, u32[]{:S(2)}) async-start(s32[64,8,1]{1,2,0:T(1,128)} %bitcast), calls=%async_computation | async-start | bytes 65536 | tf_op jit(solution)/shard_map/all_to_all | solution.py:63
  28.9 2.6 gather_fusion.1
  31.5 6.8 %all-to-all-done = s32[64,8,1]{1,2,0:T(1,128)S(1)} async-done(((s32[64,8,1]{1,2,0:T(1,128)}), s32[64,8,1]{1,2,0:T(1,128)S(1)}, u32[]{:S(2)}, u32[]{:S(2)}) %all-to-all-start) | async-done | bytes 2080 | tf_op jit(solution)/shard_map/all_to_all | solution.py:63
  38.3 4.6 %all-to-all-start.1 = ((bf16[64,8,512]{2,1,0:T(8,128)(2,1)}), bf16[64,8,512]{2,1,0:T(8,128)(2,1)S(1)}, u32[]{:S(2)}, u32[]{:S(2)}) async-start(bf16[64,8,512]{2,1,0:T(8,128)(2,1)} %bitcast.2), calls=%async_computation.1 | async-start | bytes 1048576 | tf_op jit(solution)/shard_map/all_to_all | solution.py:62
  43.0 0.0 copy-start.9
  43.0 0.0 copy-start.8
  43.0 0.5 broadcast.94
  43.5 0.7 reduce.7
  44.2 0.1 all_to_all.21
  44.3 15.8 %all-to-all-done.1 = bf16[64,8,512]{2,1,0:T(8,128)(2,1)S(1)} async-done(((bf16[64,8,512]{2,1,0:T(8,128)(2,1)}), bf16[64,8,512]{2,1,0:T(8,128)(2,1)S(1)}, u32[]{:S(2)}, u32[]{:S(2)}) %all-to-all-start.1) | async-done | bytes 524320 | tf_op jit(solution)/shard_map/all_to_all | solution.py:62
  60.2 2.5 scatter_custom_fusion
  62.7 1.5 stack.2
  64.2 4.8 %all-to-all-start.2 = ((bf16[4,512,512]{2,1,0:T(8,128)(2,1)}), bf16[4,512,512]{2,1,0:T(8,128)(2,1)S(1)}, u32[]{:S(2)}, u32[]{:S(2)}) async-start(bf16[4,512,512]{2,1,0:T(8,128)(2,1)} %stack.2), calls=%async_computation.2 | async-start | bytes 4194304 | tf_op jit(solution)/shard_map/all_to_all | solution.py:11
  69.0 0.1 reshape.155
  69.1 1.9 convert_reduce_fusion
  71.0 23.2 %all-to-all-done.2 = bf16[4,512,512]{2,1,0:T(8,128)(2,1)S(1)} async-done(((bf16[4,512,512]{2,1,0:T(8,128)(2,1)}), bf16[4,512,512]{2,1,0:T(8,128)(2,1)S(1)}, u32[]{:S(2)}, u32[]{:S(2)}) %all-to-all-start.2) | async-done | bytes 2097184 | tf_op jit(solution)/shard_map/all_to_all | solution.py:11
  94.2 1.0 slice_bitcast_fusion.1
  95.2 2.1 collective-permute-start
  97.3 1.3 collective-permute-start.1
  98.6 0.1 eq.17
  98.7 2.4 fusion.27
  101.1 0.0 collective-permute-done
  101.1 1.0 collective-permute-done.1
  102.1 2.8 pad_maximum_fusion
  104.9 7.0 %gather_fusion.2 = bf16[48,128,512]{2,1,0:T(8,128)(2,1)} fusion(bf16[24,128,512]{2,1,0:T(8,128)(2,1)} %bitcast.55, s32[1024]{0:T(1024)S(1)} %pad_clamp_fusion), kind=kCustom, calls=%fused_computation.2 | custom fusion | bytes 12583104 | tf_op jit(solution)/shard_map/gather | solution.py:72
  111.9 0.0 copy-start.11
  111.9 4.0 fusion.5
  115.9 0.0 copy-start.6
  116.0 1.7 convert_reduce_fusion.1
  117.7 0.5 fusion.3
  118.2 1.9 fusion.6
  120.1 12.3 %fusion.26 = (bf16[24,128,512]{2,0,1:T(8,128)(2,1)S(1)}, f32[24,128,512]{2,0,1:T(8,128)S(1)}) fusion(f32[48,128,512]{2,1,0:T(8,128)S(1)} %bitcast.54, s32[48]{0:T(128)S(1)} %eq.17), kind=kOutput, calls=%fused_computation.57 | convolution fusion | flops 907543680 | bytes 22020288 | tf_op jit(solution)/shard_map/en,nbf->ebf/dot_general | solution.py:102
  132.5 0.4 fusion.25
  132.9 0.1 copy.31
  133.0 9.1 %collective-permute-start.2 = (bf16[512,512]{1,0:T(8,128)(2,1)S(1)}, bf16[512,512]{1,0:T(8,128)(2,1)S(1)}, u32[]{:S(2)}, u32[]{:S(2)}) collective-permute-start(bf16[512,512]{1,0:T(8,128)(2,1)S(1)} %bitcast.60), channel_id=1, source_target_pairs={{0,4},{4,8},{8,12},{12,16},{16,20},{20,24},{24,28},{28,32},{32,36}... | collective-permute-start | bytes 1572872 | tf_op jit(solution)/shard_map/ppermute | solution.py:17
  142.1 0.1 copy.32
  142.2 1.3 collective-permute-start.3
  143.5 1.0 slice.86
  144.5 0.3 slice.87
  144.8 4.4 copy.29
  149.2 0.3 copy.30
  149.5 0.0 collective-permute-done.2
  149.5 0.0 copy-start.7
  149.5 1.1 constant_dynamic-update-slice_fusion
  150.7 2.4 fusion.12
  153.1 0.0 reduce-scatter.2.cloned.1.call-update
  153.1 0.0 copy-start.4
  153.1 0.0 all-reduce.3.cloned.1.call-start
  153.2 1.4 fusion.30
  154.6 1.4 fusion.29
  156.0 0.0 all-reduce.3.cloned.1.call-update
  156.0 0.0 copy-start.1
  156.0 83.4 %psum.23 = f32[512]{0:T(512)} all-reduce(f32[512]{0:T(512)S(1)} %get-tuple-element.33), channel_id=1, replica_groups=mesh['dom'=64,'rep'=4] {'dom','rep'}, use_global_device_ids=true, to_apply=%region_7.8 | all-reduce | flops 512 | bytes 4096 | tf_op jit(solution)/shard_map/psum | solution.py:83
  239.4 0.5 fusion.28
  239.9 0.0 reduce-scatter.2.cloned.1.call-done
  239.9 2.2 add_convert_fusion
  242.1 198.6 %all-reduce.3.cloned.1.call-done = (f32[512,512]{1,0:T(8,128)}, f32[512,512]{1,0:T(8,128)}) async-done(((f32[512,512]{1,0:T(8,128)}, f32[512,512]{1,0:T(8,128)}), (f32[512,512]{1,0:T(8,128)}, f32[512,512]{1,0:T(8,128)})) %all-reduce.3.cloned.1.call-update) | async-done | bytes 2097168 | tf_op jit(solution)/shard_map/psum | solution.py:83
  440.7 2.3 copy.44
  443.0 2.3 copy.45
  (26 shorter events, 0.1 us)
Async XLA Ops:
  8.0 108.0 %copy-start = (bf16[512,512]{1,0:T(8,128)(2,1)S(1)}, bf16[512,512]{1,0:T(8,128)(2,1)}, u32[]{:S(2)}) copy-start(bf16[512,512]{1,0:T(8,128)(2,1)} %param.19) | copy-start | bytes 1572868
  8.0 20.9 %copy-start.2 = (bf16[512,512]{1,0:T(8,128)(2,1)S(1)}, bf16[512,512]{1,0:T(8,128)(2,1)}, u32[]{:S(2)}) copy-start(bf16[512,512]{1,0:T(8,128)(2,1)} %param.13) | copy-start | bytes 1572868
  16.8 21.5 %all-to-all-start = ((s32[64,8,1]{1,2,0:T(1,128)}), s32[64,8,1]{1,2,0:T(1,128)S(1)}, u32[]{:S(2)}, u32[]{:S(2)}) async-start(s32[64,8,1]{1,2,0:T(1,128)} %bitcast), calls=%async_computation | async-start | bytes 65536 | tf_op jit(solution)/shard_map/all_to_all | solution.py:63
  38.3 21.8 %all-to-all-start.1 = ((bf16[64,8,512]{2,1,0:T(8,128)(2,1)}), bf16[64,8,512]{2,1,0:T(8,128)(2,1)S(1)}, u32[]{:S(2)}, u32[]{:S(2)}) async-start(bf16[64,8,512]{2,1,0:T(8,128)(2,1)} %bitcast.2), calls=%async_computation.1 | async-start | bytes 1048576 | tf_op jit(solution)/shard_map/all_to_all | solution.py:62
  43.0 26.1 %copy-start.9 = (s32[4,12]{1,0:T(4,128)S(1)}, s32[4,12]{1,0:T(4,128)}, u32[]{:S(2)}) copy-start(s32[4,12]{1,0:T(4,128)} %param.16) | copy-start | bytes 580
  43.0 26.1 %copy-start.8 = (s32[4,12]{1,0:T(4,128)S(1)}, s32[4,12]{1,0:T(4,128)}, u32[]{:S(2)}) copy-start(s32[4,12]{1,0:T(4,128)} %param.17) | copy-start | bytes 580
  64.2 30.0 %all-to-all-start.2 = ((bf16[4,512,512]{2,1,0:T(8,128)(2,1)}), bf16[4,512,512]{2,1,0:T(8,128)(2,1)S(1)}, u32[]{:S(2)}, u32[]{:S(2)}) async-start(bf16[4,512,512]{2,1,0:T(8,128)(2,1)} %stack.2), calls=%async_computation.2 | async-start | bytes 4194304 | tf_op jit(solution)/shard_map/all_to_all | solution.py:11
  69.0 170.9 %reduce-scatter.2.cloned.1.call-start = ((), (), s32[]{:S(2)}) async-start(), calls=%async_computation.4 | async-start | bytes 5242880 | tf_op jit(solution)/shard_map/reduce_scatter | solution.py:111
  95.2 5.9 %collective-permute-start = (bf16[512,512]{1,0:T(8,128)(2,1)}, bf16[512,512]{1,0:T(8,128)(2,1)}, u32[]{:S(2)}, u32[]{:S(2)}) collective-permute-start(bf16[512,512]{1,0:T(8,128)(2,1)} %get-tuple-element.39), channel_id=1, source_target_pairs={{0,4},{4,8},{8,12},{12,16},{16,20},{20,24},{24,28},{28,32},{32,36}... | collective-permute-start | bytes 1572872 | tf_op jit(solution)/shard_map/ppermute | solution.py:25
  97.3 4.8 %collective-permute-start.1 = (bf16[512,512]{1,0:T(8,128)(2,1)}, bf16[512,512]{1,0:T(8,128)(2,1)}, u32[]{:S(2)}, u32[]{:S(2)}) collective-permute-start(bf16[512,512]{1,0:T(8,128)(2,1)} %get-tuple-element.40), channel_id=1, source_target_pairs={{4,0},{8,4},{12,8},{16,12},{20,16},{24,20},{28,24},{32,28},{36,32}... | collective-permute-start | bytes 1572872 | tf_op jit(solution)/shard_map/ppermute | solution.py:28
  104.9 7.0 %copy-start.3 = (bf16[4,12,128,128]{3,2,1,0:T(8,128)(2,1)S(1)}, bf16[4,12,128,128]{3,2,1,0:T(8,128)(2,1)}, u32[]{:S(2)}) copy-start(bf16[4,12,128,128]{3,2,1,0:T(8,128)(2,1)} %param.15) | copy-start | bytes 4718596
  111.9 4.1 copy-start.5
  111.9 4.1 copy-start.10
  111.9 4.1 copy-start.11
  115.9 2.3 copy-start.6
  133.0 16.5 %collective-permute-start.2 = (bf16[512,512]{1,0:T(8,128)(2,1)S(1)}, bf16[512,512]{1,0:T(8,128)(2,1)S(1)}, u32[]{:S(2)}, u32[]{:S(2)}) collective-permute-start(bf16[512,512]{1,0:T(8,128)(2,1)S(1)} %bitcast.60), channel_id=1, source_target_pairs={{0,4},{4,8},{8,12},{12,16},{16,20},{20,24},{24,28},{28,32},{32,36}... | collective-permute-start | bytes 1572872 | tf_op jit(solution)/shard_map/ppermute | solution.py:17
  142.2 8.5 %collective-permute-start.3 = (bf16[512,512]{1,0:T(8,128)(2,1)S(1)}, bf16[512,512]{1,0:T(8,128)(2,1)S(1)}, u32[]{:S(2)}, u32[]{:S(2)}) collective-permute-start(bf16[512,512]{1,0:T(8,128)(2,1)S(1)} %bitcast.59), channel_id=1, source_target_pairs={{4,0},{8,4},{12,8},{16,12},{20,16},{24,20},{28,24},{32,28},{36,32}... | collective-permute-start | bytes 1572872 | tf_op jit(solution)/shard_map/ppermute | solution.py:17
  149.5 3.6 copy-start.7
  153.1 86.4 %copy-start.4 = (bf16[512,512]{1,0:T(8,128)(2,1)S(1)}, bf16[512,512]{1,0:T(8,128)(2,1)}, u32[]{:S(2)}) copy-start(bf16[512,512]{1,0:T(8,128)(2,1)} %param.18) | copy-start | bytes 1572868
  153.1 287.6 %all-reduce.3.cloned.1.call-start = ((), (), s32[]{:S(2)}) async-start(), calls=%async_computation.5 | async-start | bytes 4194304 | tf_op jit(solution)/shard_map/psum | solution.py:83
  156.0 289.2 %copy-start.1 = (bf16[512,512]{1,0:T(8,128)(2,1)S(1)}, bf16[512,512]{1,0:T(8,128)(2,1)}, u32[]{:S(2)}) copy-start(bf16[512,512]{1,0:T(8,128)(2,1)} %param.19) | copy-start | bytes 1572868
Sparse Core Ops, SparseCore 0:
  153.2 52.8 reduce-scatter.1
Sparse Core Ops, SparseCore 1:
  160.6 280.1 all-reduce.2
